TPU v7x, 256 devices: a whole 4x4x8 slice. The times are simulated.
256 devices in a mesh: px: 32 (over z, x_hi, core), py: 8 (over y, x_lo).
Axes of the slice: x: 4 (x_hi: 2, x_lo: 2; x = x_hi * 2 + x_lo), y: 4, z: 8, core: 2. Of those that a mesh axis runs over, the one named last changes fastest.
Arguments:
- table: float32 [25, 50, 1000], replicated, may hold values from -1 to 1
- charge: float32 [128, 32, 8], P('px', 'py'), may hold values from 0.1 to 1
- hit_bins: int32 [128, 32, 8], P('px', 'py'), may hold values from 0 to 49
- hit_ticks: int32 [128, 32, 8], P('px', 'py'), may hold values from 0 to 23
- active: int32 [128, 32], P('px', 'py'), may hold values 0 or 1
- measured: bfloat16 [128, 32, 1024], P('px', 'py'), may hold values from -6 to 6
- row_module: int32 [128], replicated, may hold values from 0 to 6, as said below
- col_module: int32 [32], replicated, may hold values from 0 to 4, as said below
Outputs:
- current: bfloat16 [128, 32, 1024], P('px', 'py')
- table_grad: float32 [25, 50, 1000], P(None, None, 'py')
Inputs may be any that keep to these rules, and one draw needn't show every extreme that they name: `row_module`: starts at 0 and never falls; it rises by one at 6 rows. `col_module`: starts at 0 and never falls; it rises by one at 4 columns.
All inputs are finite; a program needn't handle non-finite values. No bound on the sum of `active` on one device may be relied on, other than what follows from the above.
Results may differ from a plain program's by a relative error of at most 0.014.
Values may be sent and summed in bfloat16 or wider, within the bound.
No kernel may reach another device: no remote copies, remote signals or barrier semaphores. Data moves between devices by JAX's collectives and lax.ppermute only.
A program may use at most 128 MiB of HBM per device.

v0:
```python
import jax
import jax.numpy as jnp
from jax import lax
from jax.sharding import PartitionSpec as P

BINS = 50
SHIFTS = 24


def passed_along(block, axis, distance):
    devices = range(lax.axis_size(axis))
    route = [(i - distance, i) for i in devices if i - distance in devices]
    return lax.ppermute(block, axis, route)


def bin_charges(charge, hit_bins, hit_ticks):
    tick_hot = (hit_ticks[..., None] == jnp.arange(SHIFTS, dtype=jnp.int32)).astype(jnp.float32)
    bin_hot = (hit_bins[..., None] == jnp.arange(BINS, dtype=jnp.int32)).astype(jnp.float32)
    weighted = charge[..., None] * tick_hot
    return jnp.einsum("xyks,xykb->xysb", weighted, bin_hot).astype(jnp.bfloat16)


def gather_offsets(source, rows, cols, count_x, count_y):
    pieces = []
    for row_off in range(-2, 3):
        for col_off in range(-2, 3):
            partial_value = source[
                2 - row_off : 2 - row_off + count_x, 2 - col_off : 2 - col_off + count_y
            ]
            row_same = rows[2 - row_off : 2 - row_off + count_x] == rows[2 : 2 + count_x]
            col_same = cols[2 - col_off : 2 - col_off + count_y] == cols[2 : 2 + count_y]
            allowed = row_same[:, None] & col_same[None, :]
            pieces.append(
                jnp.where(
                    allowed[:, :, None, None], partial_value, jnp.zeros((), partial_value.dtype)
                )
            )
    return jnp.stack(pieces, 0)


def shift_sum(partial_value, ticks):
    total = jnp.zeros(partial_value.shape[:2] + (ticks + SHIFTS,), jnp.float32)
    for offset in range(SHIFTS):
        total = total + jnp.pad(
            partial_value[:, :, offset, :], ((0, 0), (0, 0), (offset, SHIFTS - offset))
        )
    return total


def windows(resid, ticks):
    return jnp.stack([resid[:, :, offset : offset + ticks] for offset in range(SHIFTS)], axis=2)


def residual_of(prediction, measured, active):
    return (
        (prediction - measured.astype(jnp.float32)) * active.astype(jnp.float32)[..., None]
    ).astype(jnp.bfloat16)


def on_device(table, charge, hit_bins, hit_ticks, active, measured, row_module, col_module):
    tile_x, tile_y = (charge.shape[0], charge.shape[1])
    ticks = table.shape[2]
    parts_y = lax.axis_size("py")
    share = ticks // parts_y
    span = share + SHIFTS - 1
    weights = table.astype(jnp.bfloat16)
    row_start = lax.axis_index("px") * tile_x
    col_start = lax.axis_index("py") * tile_y
    deposits = jnp.stack(
        [charge, hit_bins.astype(jnp.float32), hit_ticks.astype(jnp.float32)], axis=-1
    )
    band = lax.all_gather(deposits, "py", axis=1, tiled=True)
    above = passed_along(band[tile_x - 2 :], "px", 1)
    below = passed_along(band[:2], "px", -1)
    wide = jnp.concatenate([above, band, below], axis=0)
    binned = bin_charges(
        wide[..., 0], wide[..., 1].astype(jnp.int32), wide[..., 2].astype(jnp.int32)
    )
    source = jnp.pad(binned, ((0, 0), (2, 2), (0, 0), (0, 0)))
    width = source.shape[1] - 4
    rows_wide = lax.dynamic_slice_in_dim(
        jnp.pad(row_module, 2, constant_values=-1), row_start, tile_x + 4, 0
    )
    cols_all = jnp.pad(col_module, 2, constant_values=-1)
    own_source = lax.dynamic_slice_in_dim(source, col_start, tile_y + 4, 1)
    own_cols = lax.dynamic_slice_in_dim(cols_all, col_start, tile_y + 4, 0)
    stacked = gather_offsets(own_source, rows_wide, own_cols, tile_x, tile_y)
    partial_value = jnp.einsum(
        "oxysb,obt->xyst", stacked, weights, preferred_element_type=jnp.float32
    )
    prediction = shift_sum(partial_value, ticks)
    resid = residual_of(prediction, measured, active)
    sent = jnp.stack([resid[:, :, k * share : k * share + span] for k in range(parts_y)], axis=0)
    got = lax.all_to_all(sent, "py", 0, 0)
    band_resid = jnp.transpose(got, (1, 0, 2, 3)).reshape(tile_x, width, span)
    stacked_band = gather_offsets(source, rows_wide, cols_all, tile_x, width)
    gradient = jnp.einsum(
        "oxysb,xysu->obu",
        stacked_band,
        windows(band_resid, share),
        preferred_element_type=jnp.float32,
    )
    summed = lax.psum(gradient, "px")
    return (prediction.astype(jnp.bfloat16), summed / 16)


def solution(mesh):
    in_specs = (
        P(),
        P("px", "py", None),
        P("px", "py", None),
        P("px", "py", None),
        P("px", "py"),
        P("px", "py", None),
        P(),
        P(),
    )
    out_specs = (P("px", "py", None), P(None, None, "py"))
    return jax.shard_map(
        on_device, mesh=mesh, in_specs=in_specs, out_specs=out_specs, check_vma=False
    )
```

profile of v0, /device:TPU:101, one launch (start us, length us, event | category | flops | bytes accessed | tf_op | source)
XLA Modules:
  0.0 386.6 jit_solution(15461394324954869272)
XLA Ops:
  7.2 0.7 convert_bitcast_fusion
  7.9 0.7 pad_maximum_fusion.1
  8.6 22.5 %all_gather.3 = f32[4,32,8,3]{2,0,3,1:T(4,128)S(1)} all-gather(f32[4,4,8,3]{2,0,3,1:T(4,128)S(1)} %copy.144), channel_id=1, replica_groups=mesh['px'=32,'py'=8] {'py'}, dimensions={1}, use_global_device_ids=true | all-gather | bytes 13824 | tf_op jit(solution)/shard_map/all_gather | solution.py:72
  31.2 8.9 %collective-permute-start.1 = (f32[2,32,8,3]{2,0,3,1:T(2,128)S(1)}, f32[2,32,8,3]{2,0,3,1:T(2,128)S(1)}, u32[]{:S(2)}, u32[]{:S(2)}) collective-permute-start(f32[2,32,8,3]{2,0,3,1:T(2,128)S(1)} %get-tuple-element.30), channel_id=1, source_target_pairs={{8,0},{16,8},{24,16},{32,24},{40,32},{48,40},{56,48},{64,56},{72,6... | collective-permute-start | bytes 18440 | tf_op jit(solution)/shard_map/ppermute | solution.py:13
  40.1 4.6 %collective-permute-start = (f32[2,32,8,3]{2,0,3,1:T(2,128)S(1)}, f32[2,32,8,3]{2,0,3,1:T(2,128)S(1)}, u32[]{:S(2)}, u32[]{:S(2)}) collective-permute-start(f32[2,32,8,3]{2,0,3,1:T(2,128)S(1)} %get-tuple-element.29), channel_id=1, source_target_pairs={{0,8},{8,16},{16,24},{24,32},{32,40},{40,48},{48,56},{56,64},{64,7... | collective-permute-start | bytes 18440 | tf_op jit(solution)/shard_map/ppermute | solution.py:13
  44.7 0.9 slice_compare_fusion
  45.6 0.7 pad_dynamic-slice_fusion.1
  46.4 0.7 pad_dynamic-slice_fusion
  47.4 0.7 convert_element_type.92
  48.7 2.9 convolution_convert_fusion
  54.3 1.3 slice-done
  55.6 0.6 slice-done.1
  56.1 2.6 fusion
  59.2 1.2 fusion.46
  62.0 0.3 bitcast_dynamic-update-slice_fusion.18
  62.6 0.3 bitcast_dynamic-update-slice_fusion.17
  63.0 0.3 bitcast_dynamic-update-slice_fusion.16
  63.3 0.3 bitcast_dynamic-update-slice_fusion.15
  63.7 0.3 bitcast_dynamic-update-slice_fusion.14
  64.3 0.3 bitcast_dynamic-update-slice_fusion.13
  64.7 0.3 bitcast_dynamic-update-slice_fusion.12
  65.0 0.3 bitcast_dynamic-update-slice_fusion.11
  65.8 0.3 bitcast_dynamic-update-slice_fusion.9
  66.5 0.3 bitcast_dynamic-update-slice_fusion.7
  66.9 0.3 bitcast_dynamic-update-slice_fusion.6
  67.5 0.3 bitcast_dynamic-update-slice_fusion.5
  67.9 0.3 bitcast_dynamic-update-slice_fusion.4
  68.2 0.5 bitcast_dynamic-update-slice_fusion.3
  68.7 0.3 bitcast_dynamic-update-slice_fusion.2
  69.5 2.0 multiply_convert_fusion
  71.5 4.6 %copy-done.1 = bf16[25,4,32,24,50]{4,3,2,1,0:T(8,128)(2,1)} copy-done((bf16[25,4,32,24,50]{4,3,2,1,0:T(8,128)(2,1)}, bf16[25,4,32,24,50]{4,3,2,1,0:T(8,128)(2,1)S(1)}, u32[]{:S(2)}) %copy-start.1) | copy-done | bytes 7680024
  76.1 0.6 constant_dynamic-update-slice_fusion.32
  76.7 0.7 constant_dynamic-update-slice_fusion.31
  77.3 0.7 constant_dynamic-update-slice_fusion.30
  78.0 0.7 constant_dynamic-update-slice_fusion.29
  78.7 0.7 constant_dynamic-update-slice_fusion.28
  79.4 0.7 constant_dynamic-update-slice_fusion.27
  80.0 0.7 constant_dynamic-update-slice_fusion.26
  80.7 0.7 constant_dynamic-update-slice_fusion.25
  81.4 5.4 %all-to-all-start = ((bf16[8,4,4,148]{3,2,1,0:T(4,128)(2,1)}), bf16[8,4,4,148]{3,2,1,0:T(4,128)(2,1)S(1)}, u32[]{:S(2)}, u32[]{:S(2)}) async-start(bf16[8,4,4,148]{3,2,1,0:T(4,128)(2,1)} %constant_dynamic-update-slice_fusion.25), calls=%async_computation | async-start | bytes 131072 | tf_op jit(solution)/shard_map/all_to_all | solution.py:94
  86.8 1.1 bitcast_dynamic-update-slice_fusion.1
  88.0 1.1 bitcast_dynamic-update-slice_fusion
  89.1 2.9 all-to-all-done
  92.1 0.4 slice_bitcast_fusion.1
  94.0 2.6 stack.359
  96.6 12.7 %convolution_bitcast_fusion = f32[25,50,125]{2,1,0:T(8,128)} fusion(bf16[25,4,32,24,50]{4,3,2,1,0:T(8,128)(2,1)} %bitcast_dynamic-update-slice_fusion, bf16[4,32,24,125]{3,2,1,0:T(8,128)(2,1)S(1)} %stack.359), kind=kOutput, calls=%fused_computation.6 | convolution fusion | flops 960000000 | bytes 9073000 | tf_op jit(solution)/shard_map/oxysb,xysu->obu/dot_general | solution.py:97
  109.3 268.5 %all-reduce.29.cloned.1.call-done = f32[25,50,125]{2,1,0:T(8,128)} async-done(((f32[25,50,125]{2,1,0:T(8,128)}), f32[25,50,125]{2,1,0:T(8,128)}) %all-reduce.29.cloned.1.call-update) | async-done | bytes 625016 | tf_op jit(solution)/shard_map/psum | solution.py:103
  377.8 2.0 broadcast_multiply_fusion
  (110 shorter events, 8.9 us)
Async XLA Ops:
  31.2 16.9 %collective-permute-start.1 = (f32[2,32,8,3]{2,0,3,1:T(2,128)S(1)}, f32[2,32,8,3]{2,0,3,1:T(2,128)S(1)}, u32[]{:S(2)}, u32[]{:S(2)}) collective-permute-start(f32[2,32,8,3]{2,0,3,1:T(2,128)S(1)} %get-tuple-element.30), channel_id=1, source_target_pairs={{8,0},{16,8},{24,16},{32,24},{40,32},{48,40},{56,48},{64,56},{72,6... | collective-permute-start | bytes 18440 | tf_op jit(solution)/shard_map/ppermute | solution.py:13
  40.1 8.2 %collective-permute-start = (f32[2,32,8,3]{2,0,3,1:T(2,128)S(1)}, f32[2,32,8,3]{2,0,3,1:T(2,128)S(1)}, u32[]{:S(2)}, u32[]{:S(2)}) collective-permute-start(f32[2,32,8,3]{2,0,3,1:T(2,128)S(1)} %get-tuple-element.29), channel_id=1, source_target_pairs={{0,8},{8,16},{16,24},{24,32},{32,40},{40,48},{48,56},{56,64},{64,7... | collective-permute-start | bytes 18440 | tf_op jit(solution)/shard_map/ppermute | solution.py:13
  53.4 2.2 slice-start
  53.7 2.4 slice-start.1
  68.7 0.8 copy-start
  69.4 6.7 %copy-start.1 = (bf16[25,4,32,24,50]{4,3,2,1,0:T(8,128)(2,1)}, bf16[25,4,32,24,50]{4,3,2,1,0:T(8,128)(2,1)S(1)}, u32[]{:S(2)}) copy-start(bf16[25,4,32,24,50]{4,3,2,1,0:T(8,128)(2,1)S(1)} %fusion.6) | copy-start | bytes 23040004
  81.4 10.6 %all-to-all-start = ((bf16[8,4,4,148]{3,2,1,0:T(4,128)(2,1)}), bf16[8,4,4,148]{3,2,1,0:T(4,128)(2,1)S(1)}, u32[]{:S(2)}, u32[]{:S(2)}) async-start(bf16[8,4,4,148]{3,2,1,0:T(4,128)(2,1)} %constant_dynamic-update-slice_fusion.25), calls=%async_computation | async-start | bytes 131072 | tf_op jit(solution)/shard_map/all_to_all | solution.py:94
  86.8 291.0 %all-reduce.29.cloned.1.call-start = ((), (), s32[]{:S(2)}) async-start(), calls=%async_computation.1 | async-start | bytes 1433600 | tf_op jit(solution)/shard_map/psum | solution.py:103
Sparse Core Ops, SparseCore 0:
  109.4 268.2 all-reduce.28
where the time goes:
time: 387 us
  waiting for transfers between devices  271 us (70%)
  blocking collectives  22.5 us (6%)
  local copies, waits for them, and re-layouts  21.4 us (6%)
  other arithmetic  19.5 us (5%)
  starting transfers between devices  18.9 us (5%)
  matrix products  18.2 us (5%)
  between operations  14.8 us (4%)
    psum x1, waiting for transfers between devices, on_device(): summed = lax.psum(gradient, 'px')  268 us
    all_gather x1, blocking collectives, on_device(): band = lax.all_gather(deposits, 'py', axis=1, tiled=True)  22.5 us
    ppermute x2, starting transfers between devices, passed_along(): return lax.ppermute(block, axis, route)  13.4 us
    dot_general x1, matrix products, on_device(): jnp.einsum('oxysb,xysu->obu', stacked_band, windows(band_resid, share), p...  12.7 us
    unnamed x41, local copies, waits for them, and re-layouts  12.4 us
    unnamed x47, other arithmetic  10.9 us
  transfers between devices with their start and end apart: 4, of which 2 were waited for; matrix products, arithmetic and copies ran while one was open for 2% of the time, Pallas kernels for 0%

commit v1 on v0

--- a/solution.py
+++ b/solution.py
@@ -100,7 +100,7 @@
         windows(band_resid, share),
         preferred_element_type=jnp.float32,
     )
-    summed = lax.psum(gradient, "px")
+    summed = jnp.sum(lax.all_gather(gradient, "px"), axis=0)
     return (prediction.astype(jnp.bfloat16), summed / 16)
 
 

time: 387 us -> 296 us (0.76); the launches traced: 387 us -> 291 us
  waiting for transfers between devices: 271 us -> 168 us
  other arithmetic: 19.5 us -> 26.9 us
    psum x1 -> x0, waiting for transfers between devices: 268 us -> none  [on_device(): summed = lax.psum(gradient, 'px')]
    all_gather x0 -> x1, waiting for transfers between devices: none -> 165 us  [on_device(): summed = jnp.sum(lax.all_gather(gradient, 'px'), axis=0)]
    reduce_sum x0 -> x1, other arithmetic: none -> 8.52 us  [on_device(): summed = jnp.sum(lax.all_gather(gradient, 'px'), axis=0)]
where the time goes in v1:
time: 296 us; the launch traced here: 291 us
  waiting for transfers between devices  168 us (57%)
  other arithmetic  26.9 us (9%)
  blocking collectives  22.5 us (8%)
  local copies, waits for them, and re-layouts  21.4 us (7%)
  starting transfers between devices  18.9 us (6%)
  matrix products  18.2 us (6%)
  between operations  14.8 us (5%)
    all_gather x1, waiting for transfers between devices, on_device(): summed = jnp.sum(lax.all_gather(gradient, 'px'), axis=0)  165 us
    all_gather x1, blocking collectives, on_device(): band = lax.all_gather(deposits, 'py', axis=1, tiled=True)  22.5 us
    ppermute x2, starting transfers between devices, passed_along(): return lax.ppermute(block, axis, route)  13.4 us
    dot_general x1, matrix products, on_device(): jnp.einsum('oxysb,xysu->obu', stacked_band, windows(band_resid, share), p...  12.7 us
    unnamed x41, local copies, waits for them, and re-layouts  12.4 us
    unnamed x47, other arithmetic  10.9 us
    reduce_sum x1, other arithmetic, on_device(): summed = jnp.sum(lax.all_gather(gradient, 'px'), axis=0)  8.52 us
  transfers between devices with their start and end apart: 4, of which 2 were waited for; matrix products, arithmetic and copies ran while one was open for 2% of the time, Pallas kernels for 0%

profile of v1, /device:TPU:101, one launch (start us, length us, event | category | flops | bytes accessed | tf_op | source)
XLA Modules:
  0.0 290.8 jit_solution(13477713442231197206)
XLA Ops:
  7.2 0.7 convert_bitcast_fusion
  7.9 0.7 pad_maximum_fusion.1
  8.6 22.5 %all_gather.9 = f32[4,32,8,3]{2,0,3,1:T(4,128)S(1)} all-gather(f32[4,4,8,3]{2,0,3,1:T(4,128)S(1)} %copy.144), channel_id=1, replica_groups=mesh['px'=32,'py'=8] {'py'}, dimensions={1}, use_global_device_ids=true | all-gather | bytes 13824 | tf_op jit(solution)/shard_map/all_gather | solution.py:72
  31.2 8.9 %collective-permute-start.1 = (f32[2,32,8,3]{2,0,3,1:T(2,128)S(1)}, f32[2,32,8,3]{2,0,3,1:T(2,128)S(1)}, u32[]{:S(2)}, u32[]{:S(2)}) collective-permute-start(f32[2,32,8,3]{2,0,3,1:T(2,128)S(1)} %get-tuple-element.30), channel_id=1, source_target_pairs={{8,0},{16,8},{24,16},{32,24},{40,32},{48,40},{56,48},{64,56},{72,6... | collective-permute-start | bytes 18440 | tf_op jit(solution)/shard_map/ppermute | solution.py:13
  40.1 4.6 %collective-permute-start = (f32[2,32,8,3]{2,0,3,1:T(2,128)S(1)}, f32[2,32,8,3]{2,0,3,1:T(2,128)S(1)}, u32[]{:S(2)}, u32[]{:S(2)}) collective-permute-start(f32[2,32,8,3]{2,0,3,1:T(2,128)S(1)} %get-tuple-element.29), channel_id=1, source_target_pairs={{0,8},{8,16},{16,24},{24,32},{32,40},{40,48},{48,56},{56,64},{64,7... | collective-permute-start | bytes 18440 | tf_op jit(solution)/shard_map/ppermute | solution.py:13
  44.7 0.9 slice_compare_fusion
  45.6 0.7 pad_dynamic-slice_fusion.1
  46.4 0.7 pad_dynamic-slice_fusion
  47.4 0.7 convert_element_type.92
  48.7 2.9 convolution_convert_fusion
  54.3 1.3 slice-done
  55.6 0.6 slice-done.1
  56.1 2.6 fusion
  59.2 1.2 fusion.46
  62.0 0.3 bitcast_dynamic-update-slice_fusion.18
  62.6 0.3 bitcast_dynamic-update-slice_fusion.17
  63.0 0.3 bitcast_dynamic-update-slice_fusion.16
  63.3 0.3 bitcast_dynamic-update-slice_fusion.15
  63.7 0.3 bitcast_dynamic-update-slice_fusion.14
  64.3 0.3 bitcast_dynamic-update-slice_fusion.13
  64.7 0.3 bitcast_dynamic-update-slice_fusion.12
  65.0 0.3 bitcast_dynamic-update-slice_fusion.11
  66.5 0.3 bitcast_dynamic-update-slice_fusion.7
  66.9 0.3 bitcast_dynamic-update-slice_fusion.6
  67.5 0.3 bitcast_dynamic-update-slice_fusion.5
  67.9 0.3 bitcast_dynamic-update-slice_fusion.4
  68.2 0.5 bitcast_dynamic-update-slice_fusion.3
  68.7 0.3 bitcast_dynamic-update-slice_fusion.2
  69.5 2.0 multiply_convert_fusion
  71.5 4.6 %copy-done.1 = bf16[25,4,32,24,50]{4,3,2,1,0:T(8,128)(2,1)} copy-done((bf16[25,4,32,24,50]{4,3,2,1,0:T(8,128)(2,1)}, bf16[25,4,32,24,50]{4,3,2,1,0:T(8,128)(2,1)S(1)}, u32[]{:S(2)}) %copy-start.1) | copy-done | bytes 7680024
  76.1 0.6 constant_dynamic-update-slice_fusion.32
  76.7 0.7 constant_dynamic-update-slice_fusion.31
  77.3 0.7 constant_dynamic-update-slice_fusion.30
  78.0 0.7 constant_dynamic-update-slice_fusion.29
  78.7 0.7 constant_dynamic-update-slice_fusion.28
  79.4 0.7 constant_dynamic-update-slice_fusion.27
  80.0 0.7 constant_dynamic-update-slice_fusion.26
  80.7 0.7 constant_dynamic-update-slice_fusion.25
  81.4 5.4 %all-to-all-start = ((bf16[8,4,4,148]{3,2,1,0:T(4,128)(2,1)}), bf16[8,4,4,148]{3,2,1,0:T(4,128)(2,1)S(1)}, u32[]{:S(2)}, u32[]{:S(2)}) async-start(bf16[8,4,4,148]{3,2,1,0:T(4,128)(2,1)} %constant_dynamic-update-slice_fusion.25), calls=%async_computation | async-start | bytes 131072 | tf_op jit(solution)/shard_map/all_to_all | solution.py:94
  86.8 1.1 bitcast_dynamic-update-slice_fusion.1
  87.9 1.1 bitcast_dynamic-update-slice_fusion
  89.1 2.9 all-to-all-done
  92.1 0.4 slice_bitcast_fusion.1
  94.0 2.6 stack.359
  96.6 12.7 %convolution_bitcast_fusion = f32[25,50,125]{2,1,0:T(8,128)} fusion(bf16[25,4,32,24,50]{4,3,2,1,0:T(8,128)(2,1)} %bitcast_dynamic-update-slice_fusion, bf16[4,32,24,125]{3,2,1,0:T(8,128)(2,1)S(1)} %stack.359), kind=kOutput, calls=%fused_computation.6 | convolution fusion | flops 960000000 | bytes 9073000 | tf_op jit(solution)/shard_map/oxysb,xysu->obu/dot_general | solution.py:97
  109.3 165.2 %all-gather.3.cloned.1.call-done = f32[800,50,125]{2,1,0:T(8,128)} async-done(((f32[25,50,125]{2,1,0:T(8,128)}), f32[800,50,125]{2,1,0:T(8,128)}) %all-gather.3.cloned.1.call-update) | async-done | bytes 20000016 | tf_op jit(solution)/shard_map/all_gather | solution.py:103
  274.5 8.5 %reduce_sum.9 = f32[25,50,125]{2,1,0:T(8,128)S(1)} reduce(f32[32,25,50,125]{3,2,1,0:T(8,128)} %bitcast.371, f32[]{:T(128)} %constant.29.clone.1), dimensions={0}, to_apply=%region_0.1 | reduce | flops 4843750 | bytes 20625004 | tf_op jit(solution)/shard_map/reduce_sum | solution.py:103
  283.0 0.9 broadcast_multiply_fusion
  (111 shorter events, 9.3 us)
Async XLA Ops:
  31.2 16.9 %collective-permute-start.1 = (f32[2,32,8,3]{2,0,3,1:T(2,128)S(1)}, f32[2,32,8,3]{2,0,3,1:T(2,128)S(1)}, u32[]{:S(2)}, u32[]{:S(2)}) collective-permute-start(f32[2,32,8,3]{2,0,3,1:T(2,128)S(1)} %get-tuple-element.30), channel_id=1, source_target_pairs={{8,0},{16,8},{24,16},{32,24},{40,32},{48,40},{56,48},{64,56},{72,6... | collective-permute-start | bytes 18440 | tf_op jit(solution)/shard_map/ppermute | solution.py:13
  40.1 8.2 %collective-permute-start = (f32[2,32,8,3]{2,0,3,1:T(2,128)S(1)}, f32[2,32,8,3]{2,0,3,1:T(2,128)S(1)}, u32[]{:S(2)}, u32[]{:S(2)}) collective-permute-start(f32[2,32,8,3]{2,0,3,1:T(2,128)S(1)} %get-tuple-element.29), channel_id=1, source_target_pairs={{0,8},{8,16},{16,24},{24,32},{32,40},{40,48},{48,56},{56,64},{64,7... | collective-permute-start | bytes 18440 | tf_op jit(solution)/shard_map/ppermute | solution.py:13
  53.4 2.2 slice-start
  53.7 2.4 slice-start.1
  68.7 0.8 copy-start
  69.4 6.7 %copy-start.1 = (bf16[25,4,32,24,50]{4,3,2,1,0:T(8,128)(2,1)}, bf16[25,4,32,24,50]{4,3,2,1,0:T(8,128)(2,1)S(1)}, u32[]{:S(2)}) copy-start(bf16[25,4,32,24,50]{4,3,2,1,0:T(8,128)(2,1)S(1)} %fusion.6) | copy-start | bytes 23040004
  81.4 10.6 %all-to-all-start = ((bf16[8,4,4,148]{3,2,1,0:T(4,128)(2,1)}), bf16[8,4,4,148]{3,2,1,0:T(4,128)(2,1)S(1)}, u32[]{:S(2)}, u32[]{:S(2)}) async-start(bf16[8,4,4,148]{3,2,1,0:T(4,128)(2,1)} %constant_dynamic-update-slice_fusion.25), calls=%async_computation | async-start | bytes 131072 | tf_op jit(solution)/shard_map/all_to_all | solution.py:94
  86.8 187.7 %all-gather.3.cloned.1.call-start = ((), (), s32[]{:S(2)}) async-start(), calls=%async_computation.1 | async-start | bytes 23654400 | tf_op jit(solution)/shard_map/all_gather | solution.py:103
Sparse Core Ops, SparseCore 0:
  109.4 165.0 all-gather.2
